TPU v7x, 256 devices: a whole 4x4x8 slice. The times are simulated.
256 devices in a mesh: group: 8 (over x, y_lo), tp: 32 (over z, y_hi, core).
Axes of the slice: x: 4, y: 4 (y_hi: 2, y_lo: 2; y = y_hi * 2 + y_lo), z: 8, core: 2. Of those that a mesh axis runs over, the one named last changes fastest.
Arguments:
- hidden: bfloat16 [2, 256, 8192], P(None, 'group', 'tp'), may hold values from -6 to 6
- query_weight: bfloat16 [8192, 4096], P(None, 'tp'), may hold values from -0.0625 to 0.0625
- key_value_weight: bfloat16 [8192, 1024], P('tp'), may hold values from -0.0625 to 0.0625
- output_weight: bfloat16 [4096, 8192], P('tp'), may hold values from -0.1875 to 0.1875
- adapter_down_weight: bfloat16 [32, 8192, 128], P('group', 'tp'), may hold values from -0.0625 to 0.0625
- adapter_up_query: bfloat16 [32, 64, 4096], P('group', None, 'tp'), may hold values from -0.75 to 0.75
- adapter_up_value: bfloat16 [32, 64, 512], P('group'), may hold values from -0.75 to 0.75
- key_value_pool: bfloat16 [8192, 16, 1024], P(('group', 'tp')), may hold values from -250 to 250
- lengths: int32 [256], P(('group', 'tp')), may hold values from 257 to 512
- request_page_table: int32 [256, 32], P(('group', 'tp')), may hold values from 0 to 63, as said below
- page_send_list: int32 [8, 32, 8, 4], P('group', 'tp'), may hold values from -1 to 31, as said below
- request_adapter_entry: int32 [256], P('group'), may hold values from 0 to 15, as said below
- read_rows_list: int32 [8, 8, 2], replicated, may hold values from -1 to 3, as said below
Outputs:
- layer_out: bfloat16 [2, 256, 8192], P(None, 'group', 'tp')
Inputs may be any that keep to these rules, and one draw needn't show every extreme that they name: `request_page_table`: the entries of one device's requests are distinct; an entry below 32 names a page of that device's pool, an entry 32 + g * 4 + c names slot c of what device (g, same column) lists for this group in page_send_list, and only listed slots are named. `page_send_list`: for each source device and target group the listed pages are distinct and fill the first slots, -1 marks an empty slot; a group lists nothing for itself; in every draw each device fills all 4 slots for some group. `request_adapter_entry`: entry e of a request of group h names slot e % 2 of read_rows_list[h, e // 2], never an empty one; every listed slot is named by some request of the group. `read_rows_list`: listed rows of one reading group and owner are distinct and fill the first slots, -1 marks an empty slot; every reading group reads 2 adapters from some owner.
All inputs are finite; a program needn't handle non-finite values.
Results may differ from a plain program's by a relative error of at most 0.0158.
The roundings to bfloat16 on the way count: a program that leaves them out, or rounds other values in their place, can miss the bound.
Values may be sent and summed in bfloat16 or wider, within the bound.
No kernel may reach another device: no remote copies, remote signals or barrier semaphores. Data moves between devices by JAX's collectives and lax.ppermute only.
A program may use at most 64 MiB of HBM per device.

v0:
```python
import math
import jax
import jax.numpy as jnp
from jax import lax
from jax.sharding import PartitionSpec as P

HEAD_SIZE = 128
QUERY_HEADS = 32
KEY_VALUE_HEADS = 4
ADAPTER_RANK = 64
ADAPTER_SCALE = 1.5


def attend(query_own, ctx_pages, keyval_new, lengths):
    key_span_width = KEY_VALUE_HEADS * HEAD_SIZE
    group_q = QUERY_HEADS // KEY_VALUE_HEADS
    step_count = query_own.shape[0]
    batch_own = query_own.shape[1]
    ctx_len = ctx_pages.shape[1]
    query_rows = query_own.reshape(step_count, batch_own, KEY_VALUE_HEADS, group_q, HEAD_SIZE)
    ctx_keys = ctx_pages[..., :key_span_width].reshape(
        batch_own, ctx_len, KEY_VALUE_HEADS, HEAD_SIZE
    )
    ctx_values = ctx_pages[..., key_span_width:].reshape(
        batch_own, ctx_len, KEY_VALUE_HEADS, HEAD_SIZE
    )
    new_keys = keyval_new[..., :key_span_width].reshape(
        batch_own, step_count, KEY_VALUE_HEADS, HEAD_SIZE
    )
    new_values = keyval_new[..., key_span_width:].reshape(
        batch_own, step_count, KEY_VALUE_HEADS, HEAD_SIZE
    )
    score_scale = 1.0 / math.sqrt(HEAD_SIZE)
    ctx_scores = (
        jnp.einsum("sbkgd,bckd->bkgsc", query_rows, ctx_keys, preferred_element_type=jnp.float32)
        * score_scale
    )
    new_scores = (
        jnp.einsum("sbkgd,btkd->bkgst", query_rows, new_keys, preferred_element_type=jnp.float32)
        * score_scale
    )
    ctx_mask = (jnp.arange(ctx_len)[None, :] < lengths[:, None])[:, None, None, None, :]
    new_mask = jnp.arange(step_count)[None, :] <= jnp.arange(step_count)[:, None]
    ctx_scores = jnp.where(ctx_mask, ctx_scores, -jnp.inf)
    new_scores = jnp.where(new_mask, new_scores, -jnp.inf)
    row_max = jnp.maximum(
        jnp.max(ctx_scores, -1, keepdims=True), jnp.max(new_scores, -1, keepdims=True)
    )
    ctx_weights = jnp.exp(ctx_scores - row_max)
    new_weights = jnp.exp(new_scores - row_max)
    totals = jnp.sum(ctx_weights, -1, keepdims=True) + jnp.sum(new_weights, -1, keepdims=True)
    context = jnp.einsum(
        "bkgsc,bckd->bkgsd",
        ctx_weights.astype(jnp.bfloat16),
        ctx_values,
        preferred_element_type=jnp.float32,
    )
    context = context + jnp.einsum(
        "bkgst,btkd->bkgsd",
        new_weights.astype(jnp.bfloat16),
        new_values,
        preferred_element_type=jnp.float32,
    )
    context = context / totals
    return (
        jnp.transpose(context, (3, 0, 1, 2, 4))
        .reshape(step_count, batch_own, QUERY_HEADS, HEAD_SIZE)
        .astype(jnp.bfloat16)
    )


def per_device(
    hidden,
    query_weight,
    key_value_weight,
    output_weight,
    adapter_down_weight,
    adapter_up_query,
    adapter_up_value,
    key_value_pool,
    lengths,
    request_page_table,
    page_send_list,
    request_adapter_entry,
    read_rows_list,
):
    group_number = lax.axis_index("group")
    column_id = lax.axis_index("tp")
    step_count, batch_rows, width_local = hidden.shape
    batch_own = lengths.shape[0]
    key_span_width = KEY_VALUE_HEADS * HEAD_SIZE
    cap_slots = read_rows_list.shape[2]
    holder_group = request_adapter_entry // cap_slots
    slot_column = request_adapter_entry % cap_slots
    own_start = column_id * batch_own
    whole_down, whole_upq, whole_upv = (
        lax.all_gather(adapter_down_weight, "group", axis=0, tiled=True),
        lax.all_gather(adapter_up_query, "group", axis=0, tiled=True),
        lax.all_gather(adapter_up_value, "group", axis=0, tiled=True),
    )
    storage_rows = (
        holder_group * adapter_down_weight.shape[0]
        + read_rows_list[group_number, holder_group, slot_column]
    )
    down_rows = jnp.take(whole_down, storage_rows, axis=0)
    upq_rows = jnp.take(whole_upq, storage_rows, axis=0)
    upv_rows = jnp.take(
        whole_upv, lax.dynamic_slice_in_dim(storage_rows, own_start, batch_own), axis=0
    )
    shrink_part = jnp.einsum("srd,rdk->srk", hidden, down_rows, preferred_element_type=jnp.float32)
    down_projected_low = lax.psum(shrink_part, "tp").astype(jnp.bfloat16)
    query_plain = jnp.einsum(
        "srd,dc->src",
        lax.all_gather(hidden, "tp", axis=2, tiled=True),
        query_weight,
        preferred_element_type=jnp.float32,
    )
    query_adapter_term = jnp.einsum(
        "srk,rkc->src",
        down_projected_low[..., :ADAPTER_RANK],
        upq_rows,
        preferred_element_type=jnp.float32,
    )
    query_rows = (query_plain + ADAPTER_SCALE * query_adapter_term).astype(jnp.bfloat16)
    key_value_plain = lax.psum_scatter(
        jnp.einsum("srd,dc->rsc", hidden, key_value_weight, preferred_element_type=jnp.float32),
        "tp",
        scatter_dimension=0,
        tiled=True,
    )
    shrink_own = lax.dynamic_slice_in_dim(down_projected_low, own_start, batch_own, 1)
    value_adapter_term = ADAPTER_SCALE * jnp.einsum(
        "srk,rkc->rsc", shrink_own[..., ADAPTER_RANK:], upv_rows, preferred_element_type=jnp.float32
    )
    keyval_new = jnp.concatenate(
        [
            key_value_plain[..., :key_span_width],
            key_value_plain[..., key_span_width:] + value_adapter_term,
        ],
        -1,
    ).astype(jnp.bfloat16)
    heads_local = query_rows.shape[2] // HEAD_SIZE
    query_own = lax.all_to_all(
        query_rows.reshape(step_count, batch_rows, heads_local, HEAD_SIZE),
        "tp",
        split_axis=1,
        concat_axis=2,
        tiled=True,
    )
    move_row = page_send_list[0, 0]
    present_pages = (move_row >= 0).reshape(-1)
    outgoing = (
        jnp.take(key_value_pool, jnp.maximum(move_row, 0).reshape(-1), axis=0)
        * present_pages.astype(key_value_pool.dtype)[:, None, None]
    )
    arrived_pages = lax.all_to_all(outgoing, "group", split_axis=0, concat_axis=0, tiled=True)
    combined = jnp.concatenate([key_value_pool, arrived_pages], 0)
    ctx_pages = jnp.take(combined, request_page_table.reshape(-1), axis=0).reshape(
        batch_own, -1, 2 * key_span_width
    )
    attended = attend(query_own, ctx_pages, keyval_new, lengths)
    heads_back = lax.all_to_all(attended, "tp", split_axis=2, concat_axis=1, tiled=True)
    projected = jnp.dot(
        heads_back.reshape(step_count * batch_rows, -1),
        output_weight,
        preferred_element_type=jnp.float32,
    )
    summed = lax.psum_scatter(
        projected.reshape(step_count, batch_rows, -1), "tp", scatter_dimension=2, tiled=True
    )
    return summed.astype(jnp.bfloat16)


def solution(mesh):
    placed = (
        P(None, "group", "tp"),
        P(None, "tp"),
        P("tp", None),
        P("tp", None),
        P("group", "tp", None),
        P("group", None, "tp"),
        P("group", None, None),
        P(("group", "tp"), None, None),
        P(("group", "tp")),
        P(("group", "tp"), None),
        P("group", "tp", None, None),
        P("group"),
        P(),
    )
    return jax.shard_map(
        per_device, mesh=mesh, in_specs=placed, out_specs=P(None, "group", "tp"), check_vma=False
    )
```

profile of v0, /device:TPU:6, one launch (start us, length us, event | category | flops | bytes accessed | tf_op | source)
XLA Modules:
  0.0 627.6 jit_solution(2606935624223614851)
XLA Ops:
  6.5 0.7 all-gather.6.cloned.1.call-update
  7.3 0.7 all-gather.4.cloned.1.call-update
  8.1 1.2 convolution_bitcast_fusion
  9.3 0.9 copy.70
  10.3 0.7 compare_convert_fusion
  11.0 0.7 broadcast_maximum_fusion
  11.6 0.1 copy.62
  11.7 0.1 reshape.312
  11.8 0.1 copy.60
  11.9 0.1 le.59
  12.0 0.1 copy.61
  12.1 0.1 reshape.322
  12.2 1.8 gather_fusion
  14.1 1.1 select_multiply_fusion
  15.2 6.5 %all-to-all-start = ((bf16[32,16,1024]{2,1,0:T(8,128)(2,1)}), bf16[32,16,1024]{2,1,0:T(8,128)(2,1)}, u32[]{:S(2)}, u32[]{:S(2)}) async-start(bf16[32,16,1024]{2,1,0:T(8,128)(2,1)} %select_multiply_fusion), calls=%async_computation | async-start | bytes 2097152 | tf_op jit(solution)/shard_map/all_to_all | solution.py:156
  21.7 0.6 all-gather.8.cloned.1.call-update
  22.3 0.8 gather_fusion.2
  23.2 0.1 broadcast_in_dim.98
  23.3 0.1 broadcast_in_dim.99
  24.0 0.6 dynamic_slice.7
  26.6 47.8 %all_gather.13 = bf16[32,64,128]{2,1,0:T(8,128)(2,1)} all-gather(bf16[4,64,128]{2,1,0:T(8,128)(2,1)S(1)} %copy-done.4), channel_id=1, replica_groups=mesh['group'=8,'tp'=32] {'group'}, dimensions={0}, use_global_device_ids=true | all-gather | bytes 589824 | tf_op jit(solution)/shard_map/all_gather | solution.py:98
  74.4 2.5 gather_fusion.3
  76.8 0.6 dynamic-slice.4
  77.5 2.7 pad_maximum_fusion
  80.2 2.2 gather_fusion.1
  82.4 1.3 copy.63
  83.8 1.3 broadcast_select_fusion
  85.1 0.1 fusion.82
  85.2 3.7 gather_fusion.4
  88.9 2.0 fusion.10
  91.0 134.4 %psum.7 = bf16[2,32,128]{2,0,1:T(2,128)(2,1)S(1)} all-reduce(f32[2,32,128]{2,0,1:T(2,128)S(1)} %fusion.10), channel_id=1, replica_groups=mesh['group'=8,'tp'=32] {'tp'}, use_global_device_ids=true, to_apply=%region_0.1 | all-reduce | flops 8192 | bytes 49152 | tf_op jit(solution)/shard_map/psum | solution.py:111
  225.4 1.3 fusion.31
  226.7 2.4 fusion.21
  229.2 0.6 copy.66
  229.8 3.8 all-to-all-start.1
  233.7 196.1 %all-reduce.3.cloned.1.call-done = f32[32,2,1024]{2,1,0:T(2,128)} async-done(((f32[32,2,1024]{2,1,0:T(2,128)}), f32[32,2,1024]{2,1,0:T(2,128)}) %all-reduce.3.cloned.1.call-update) | async-done | bytes 262160
  429.8 1.5 convolution_multiply_fusion.1
  431.3 0.1 fusion.81
  431.3 0.3 fusion.83
  431.6 0.2 fusion.35
  431.8 0.1 fusion.55
  431.9 0.3 fusion.38
  432.2 51.4 %all-gather.8.cloned.1.call-done = bf16[32,64,512]{2,1,0:T(8,128)(2,1)} async-done(((bf16[4,64,512]{2,1,0:T(8,128)(2,1)}), bf16[32,64,512]{2,1,0:T(8,128)(2,1)}) %all-gather.8.cloned.1.call-update) | async-done | bytes 2097168 | tf_op jit(solution)/shard_map/all_gather | solution.py:99
  483.6 1.8 fusion.24
  485.4 19.1 %all_to_all.23 = bf16[2,1,32,128]{3,0,1,2:T(2,128)(2,1)S(1)} all-to-all(bf16[2,1,32,128]{3,0,1,2:T(2,128)(2,1)S(1)} %copy.79), channel_id=1, replica_groups=mesh['group'=8,'tp'=32] {'tp'}, dimensions={2} | all-to-all | bytes 32768 | tf_op jit(solution)/shard_map/all_to_all | solution.py:162
  504.5 1.8 fusion
  506.3 113.3 %reduce-scatter.2.cloned.1.call-done = f32[2,32,256]{2,1,0:T(8,128)} async-done(((f32[2,32,8192]{2,1,0:T(8,128)}), f32[2,32,256]{2,1,0:T(8,128)}) %reduce-scatter.2.cloned.1.call-update) | async-done | bytes 65552 | tf_op jit(solution)/shard_map/reduce_scatter | solution.py:168
  619.6 1.5 convert_element_type.64
  (42 shorter events, 0.4 us)
Async XLA Ops:
  6.5 498.0 %copy-start = (bf16[128,8192]{1,0:T(8,128)(2,1)S(1)}, bf16[128,8192]{1,0:T(8,128)(2,1)}, u32[]{:S(2)}) copy-start(bf16[128,8192]{1,0:T(8,128)(2,1)} %param.16) | copy-start | bytes 6291460
  6.5 78.7 %all-gather.6.cloned.1.call-start = ((), (), s32[]{:S(2)}) async-start(), calls=%async_computation.5 | async-start | bytes 2359296 | tf_op jit(solution)/shard_map/all_gather | solution.py:97
  7.3 219.5 %all-gather.4.cloned.1.call-start = ((), (), s32[]{:S(2)}) async-start(), calls=%async_computation.4 | async-start | bytes 1081344 | tf_op jit(solution)/shard_map/all_gather | solution.py:114
  8.0 421.8 %all-reduce.3.cloned.1.call-start = ((), (), s32[]{:S(2)}) async-start(), calls=%async_computation.8 | async-start | bytes 524288
  14.0 8.3 %copy-start.5 = (s32[32]{0:T(128)S(1)}, s32[32]{0:T(128)}, u32[]{:S(2)}) copy-start(s32[32]{0:T(128)} %param.24) | copy-start | bytes 388
  14.0 8.3 %copy-start.1 = (s32[8,8,2]{1,2,0:T(2,128)S(1)}, s32[8,8,2]{1,2,0:T(2,128)}, u32[]{:S(2)}) copy-start(s32[8,8,2]{1,2,0:T(2,128)} %param.25) | copy-start | bytes 1540
  14.1 9.1 %copy-start.6 = (s32[1,32]{1,0:T(1,128)S(1)}, s32[1,32]{1,0:T(1,128)}, u32[]{:S(2)}) copy-start(s32[1,32]{1,0:T(1,128)} %param.22) | copy-start | bytes 388
  14.1 12.5 %copy-start.4 = (bf16[4,64,128]{2,1,0:T(8,128)(2,1)S(1)}, bf16[4,64,128]{2,1,0:T(8,128)(2,1)}, u32[]{:S(2)}) copy-start(bf16[4,64,128]{2,1,0:T(8,128)(2,1)} %param.18) | copy-start | bytes 196612
  15.2 61.6 %copy-start.7 = (u32[256]{0:T(256)S(1)}, u32[256]{0:T(256)}, u32[]{:S(2)}) copy-start(u32[256]{0:T(256)} %constant.176) | copy-start | bytes 3076
  15.2 62.3 %copy-start.2 = (bf16[32,16,1024]{2,1,0:T(8,128)(2,1)S(1)}, bf16[32,16,1024]{2,1,0:T(8,128)(2,1)}, u32[]{:S(2)}) copy-start(bf16[32,16,1024]{2,1,0:T(8,128)(2,1)} %param.20) | copy-start | bytes 3145732
  15.2 62.2 %all-to-all-start = ((bf16[32,16,1024]{2,1,0:T(8,128)(2,1)}), bf16[32,16,1024]{2,1,0:T(8,128)(2,1)}, u32[]{:S(2)}, u32[]{:S(2)}) async-start(bf16[32,16,1024]{2,1,0:T(8,128)(2,1)} %select_multiply_fusion), calls=%async_computation | async-start | bytes 2097152 | tf_op jit(solution)/shard_map/all_to_all | solution.py:156
  21.7 461.9 %all-gather.8.cloned.1.call-start = ((), (), s32[]{:S(2)}) async-start(), calls=%async_computation.6 | async-start | bytes 2359296 | tf_op jit(solution)/shard_map/all_gather | solution.py:99
  85.2 3.8 copy-start.3
  229.8 200.0 %all-to-all-start.1 = ((bf16[2,32,1,128]{3,0,2,1:T(2,128)(2,1)}), bf16[2,32,1,128]{3,0,2,1:T(2,128)(2,1)S(1)}, u32[]{:S(2)}, u32[]{:S(2)}) async-start(bf16[2,32,1,128]{3,0,2,1:T(2,128)(2,1)} %copy.66), calls=%async_computation.1 | async-start | bytes 32768 | tf_op jit(solution)/shard_map/all_to_all | solution.py:143
  233.6 386.0 %reduce-scatter.2.cloned.1.call-start = ((), (), s32[]{:S(2)}) async-start(), calls=%async_computation.7 | async-start | bytes 2162688 | tf_op jit(solution)/shard_map/reduce_scatter | solution.py:168
Sparse Core Ops, SparseCore 0:
  9.1 74.8 all-gather.5
  86.6 76.9 all-gather.3
  166.2 263.5 all-reduce.2
  431.6 52.0 all-gather.7
  506.4 113.1 reduce-scatter.1
where the time goes:
time: 628 us
  waiting for transfers between devices  363 us (58%)
  blocking collectives  201 us (32%)
  local copies, waits for them, and re-layouts  16 us (3%)
  between operations  16 us (3%)
  matrix products  12.6 us (2%)
  starting transfers between devices  10.5 us (2%)
  other arithmetic  8.48 us (1%)
    unnamed x6, waiting for transfers between devices  198 us
    psum x1, blocking collectives, per_device(): down_projected_low = lax.psum(shrink_part, 'tp').astype(jnp.bfloat16)  134 us
    reduce_scatter x1, waiting for transfers between devices, per_device(): lax.psum_scatter(projected.reshape(step_count, batch_rows, -1), 'tp', sca...  113 us
    all_gather x1, waiting for transfers between devices, per_device(): lax.all_gather(adapter_up_value, 'group', axis=0, tiled=True)  51.4 us
    all_gather x1, blocking collectives, per_device(): lax.all_gather(adapter_up_query, 'group', axis=0, tiled=True)  47.8 us
    all_to_all x1, blocking collectives, per_device(): lax.all_to_all(attended, 'tp', split_axis=2, concat_axis=1, tiled=True)  19.1 us
  transfers between devices with their start and end apart: 7, of which 3 were waited for; matrix products, arithmetic and copies ran while one was open for 5% of the time, Pallas kernels for 0%

commit v1 on v0

--- a/solution.py
+++ b/solution.py
@@ -108,7 +108,7 @@
         whole_upv, lax.dynamic_slice_in_dim(storage_rows, own_start, batch_own), axis=0
     )
     shrink_part = jnp.einsum("srd,rdk->srk", hidden, down_rows, preferred_element_type=jnp.float32)
-    down_projected_low = lax.psum(shrink_part, "tp").astype(jnp.bfloat16)
+    down_projected_low = jnp.sum(lax.all_gather(shrink_part, "tp"), axis=0).astype(jnp.bfloat16)
     query_plain = jnp.einsum(
         "srd,dc->src",
         lax.all_gather(hidden, "tp", axis=2, tiled=True),

time: 628 us -> 691 us (1.10)
  waiting for transfers between devices: 363 us -> 567 us
  blocking collectives: 201 us -> 56.4 us
    psum x1 -> x0, blocking collectives: 134 us -> none  [per_device(): down_projected_low = lax.psum(shrink_part, 'tp').astype(jnp.bfloat16)]
    all_gather x1, waiting for transfers between devices: 0.02 us -> 68.9 us  [per_device(): lax.all_gather(hidden, 'tp', axis=2, tiled=True)]
    unnamed x6 -> x7, waiting for transfers between devices: 198 us -> 259 us
    all_gather x1, waiting for transfers between devices: 0.02 us -> 55.5 us  [per_device(): lax.all_gather(adapter_down_weight, 'group', axis=0, tiled=True)]
    all_gather x0 -> x1, waiting for transfers between devices: none -> 19.6 us  [per_device(): lax.all_gather(shrink_part, 'tp')]
    all_gather x1, blocking collectives: 47.8 us -> 37.3 us  [per_device(): lax.all_gather(adapter_up_query, 'group', axis=0, tiled=True)]
  transfers between devices with their start and end apart: 7 -> 8, of which waited for: 3 -> 6; matrix products, arithmetic and copies ran while one was open for 5% -> 4% of each run, Pallas kernels for 0% -> 0%
where the time goes in v1:
time: 691 us; the launch traced here: 690 us
  waiting for transfers between devices  567 us (82%)
  blocking collectives  56.4 us (8%)
  local copies, waits for them, and re-layouts  17.3 us (3%)
  between operations  16 us (2%)
  starting transfers between devices  12.4 us (2%)
  matrix products  11.5 us (2%)
  other arithmetic  9.08 us (1%)
    unnamed x7, waiting for transfers between devices  259 us
    reduce_scatter x1, waiting for transfers between devices, per_device(): lax.psum_scatter(projected.reshape(step_count, batch_rows, -1), 'tp', sca...  113 us
    all_gather x1, waiting for transfers between devices, per_device(): lax.all_gather(hidden, 'tp', axis=2, tiled=True)  68.9 us
    all_gather x1, waiting for transfers between devices, per_device(): lax.all_gather(adapter_down_weight, 'group', axis=0, tiled=True)  55.5 us
    all_gather x1, waiting for transfers between devices, per_device(): lax.all_gather(adapter_up_value, 'group', axis=0, tiled=True)  51.5 us
    all_gather x1, blocking collectives, per_device(): lax.all_gather(adapter_up_query, 'group', axis=0, tiled=True)  37.3 us
    all_gather x1, waiting for transfers between devices, per_device(): lax.all_gather(shrink_part, 'tp')  19.6 us
    all_to_all x1, blocking collectives, per_device(): lax.all_to_all(attended, 'tp', split_axis=2, concat_axis=1, tiled=True)  19.1 us
  transfers between devices with their start and end apart: 8, of which 6 were waited for; matrix products, arithmetic and copies ran while one was open for 4% of the time, Pallas kernels for 0%

profile of v1, /device:TPU:6, one launch (start us, length us, event | category | flops | bytes accessed | tf_op | source)
XLA Modules:
  0.0 690.0 jit_solution(8702371679187426277)
XLA Ops:
  6.5 0.7 all-gather.8.cloned.1.call-update
  7.3 0.7 fusion.65
  8.0 1.5 gather_fusion.2
  9.5 55.5 %all-gather.8.cloned.1.call-done = bf16[32,256,128]{2,1,0:T(8,128)(2,1)} async-done(((bf16[4,256,128]{2,1,0:T(8,128)(2,1)}), bf16[32,256,128]{2,1,0:T(8,128)(2,1)}) %all-gather.8.cloned.1.call-update) | async-done | bytes 2097168 | tf_op jit(solution)/shard_map/all_gather | solution.py:97
  65.0 3.7 gather_fusion.4
  68.8 2.1 fusion.10
  70.9 0.6 copy.88
  71.6 0.7 all-gather.6.cloned.1.call-update
  72.4 0.2 convolution_bitcast_fusion
  72.6 0.9 copy.95
  73.6 0.5 all-gather.10.cloned.1.call-update
  74.2 0.1 copy.85
  74.3 0.1 reshape.312
  74.3 0.1 copy.83
  74.4 0.1 le.59
  74.6 0.1 reshape.322
  74.7 1.8 gather_fusion
  76.6 1.1 select_multiply_fusion
  77.7 5.8 all-to-all-start
  83.5 37.3 %all_gather.19 = bf16[32,64,128]{2,1,0:T(8,128)(2,1)} all-gather(bf16[4,64,128]{2,1,0:T(8,128)(2,1)S(1)} %copy-done.5), channel_id=1, replica_groups=mesh['group'=8,'tp'=32] {'group'}, dimensions={0}, use_global_device_ids=true | all-gather | bytes 589824 | tf_op jit(solution)/shard_map/all_gather | solution.py:98
  120.8 2.5 gather_fusion.3
  123.3 0.1 broadcast_in_dim.99
  124.1 0.6 dynamic_slice.7
  126.3 0.6 dynamic-slice.4
  126.9 2.7 pad_maximum_fusion
  129.7 2.2 gather_fusion.1
  131.9 1.3 copy.86
  133.2 1.3 broadcast_select_fusion
  134.6 19.6 %all-gather.12.cloned.1.call-done = f32[64,32,128]{2,1,0:T(8,128)} async-done(((f32[2,32,128]{2,1,0:T(8,128)}), f32[64,32,128]{2,1,0:T(8,128)}) %all-gather.12.cloned.1.call-update) | async-done | bytes 1048592 | tf_op jit(solution)/shard_map/all_gather | solution.py:111
  154.3 1.3 reduce_sum.27
  155.6 1.3 fusion.31
  156.9 68.9 %all-gather.6.cloned.1.call-done = bf16[2,32,8192]{2,1,0:T(8,128)(2,1)} async-done(((bf16[2,32,256]{2,1,0:T(8,128)(2,1)}), bf16[2,32,8192]{2,1,0:T(8,128)(2,1)}) %all-gather.6.cloned.1.call-update) | async-done | bytes 1048592 | tf_op jit(solution)/shard_map/all_gather | solution.py:114
  225.8 2.4 fusion.21
  228.2 0.6 copy.91
  228.8 6.4 all-to-all-start.1
  235.3 256.7 %all-reduce.3.cloned.1.call-done = f32[32,2,1024]{2,1,0:T(2,128)} async-done(((f32[32,2,1024]{2,1,0:T(2,128)}), f32[32,2,1024]{2,1,0:T(2,128)}) %all-reduce.3.cloned.1.call-update) | async-done | bytes 262160
  492.0 1.4 convolution_multiply_fusion.1
  493.4 0.1 fusion.81
  493.5 0.3 fusion.83
  493.8 0.2 fusion.35
  494.0 0.1 fusion.55
  494.1 0.3 fusion.38
  494.4 51.5 %all-gather.10.cloned.1.call-done = bf16[32,64,512]{2,1,0:T(8,128)(2,1)} async-done(((bf16[4,64,512]{2,1,0:T(8,128)(2,1)}), bf16[32,64,512]{2,1,0:T(8,128)(2,1)}) %all-gather.10.cloned.1.call-update) | async-done | bytes 2097168 | tf_op jit(solution)/shard_map/all_gather | solution.py:99
  545.8 1.7 fusion.24
  547.6 19.1 %all_to_all.23 = bf16[2,1,32,128]{3,0,1,2:T(2,128)(2,1)S(1)} all-to-all(bf16[2,1,32,128]{3,0,1,2:T(2,128)(2,1)S(1)} %copy.104), channel_id=1, replica_groups=mesh['group'=8,'tp'=32] {'tp'}, dimensions={2} | all-to-all | bytes 32768 | tf_op jit(solution)/shard_map/all_to_all | solution.py:162
  566.7 1.8 fusion
  568.5 113.3 %reduce-scatter.2.cloned.1.call-done = f32[2,32,256]{2,1,0:T(8,128)} async-done(((f32[2,32,8192]{2,1,0:T(8,128)}), f32[2,32,256]{2,1,0:T(8,128)}) %reduce-scatter.2.cloned.1.call-update) | async-done | bytes 65552 | tf_op jit(solution)/shard_map/reduce_scatter | solution.py:168
  681.7 1.5 convert_element_type.64
  (49 shorter events, 0.7 us)
Async XLA Ops:
  6.5 560.2 %copy-start = (bf16[128,8192]{1,0:T(8,128)(2,1)S(1)}, bf16[128,8192]{1,0:T(8,128)(2,1)}, u32[]{:S(2)}) copy-start(bf16[128,8192]{1,0:T(8,128)(2,1)} %param.16) | copy-start | bytes 6291460
  6.5 58.5 %all-gather.8.cloned.1.call-start = ((), (), s32[]{:S(2)}) async-start(), calls=%async_computation.5 | async-start | bytes 2359296 | tf_op jit(solution)/shard_map/all_gather | solution.py:97
  7.3 147.0 %all-gather.12.cloned.1.call-start = ((), (), s32[]{:S(2)}) async-start(), calls=%async_computation.8 | async-start | bytes 1081344 | tf_op jit(solution)/shard_map/all_gather | solution.py:111
  9.5 59.3 %copy-start.3 = (bf16[2,32,256]{2,1,0:T(8,128)(2,1)S(1)}, bf16[2,32,256]{2,1,0:T(8,128)(2,1)}, u32[]{:S(2)}) copy-start(bf16[2,32,256]{2,1,0:T(8,128)(2,1)} %param.13) | copy-start | bytes 98308
  68.8 3.6 copy-start.2
  68.8 3.6 copy-start.4
  68.8 5.3 copy-start.6
  71.5 154.2 %all-gather.6.cloned.1.call-start = ((), (), s32[]{:S(2)}) async-start(), calls=%async_computation.4 | async-start | bytes 1081344 | tf_op jit(solution)/shard_map/all_gather | solution.py:114
  72.3 419.7 %all-reduce.3.cloned.1.call-start = ((), (), s32[]{:S(2)}) async-start(), calls=%async_computation.9 | async-start | bytes 524288
  73.5 472.3 %all-gather.10.cloned.1.call-start = ((), (), s32[]{:S(2)}) async-start(), calls=%async_computation.6 | async-start | bytes 2359296 | tf_op jit(solution)/shard_map/all_gather | solution.py:99
  76.6 6.9 %copy-start.5 = (bf16[4,64,128]{2,1,0:T(8,128)(2,1)S(1)}, bf16[4,64,128]{2,1,0:T(8,128)(2,1)}, u32[]{:S(2)}) copy-start(bf16[4,64,128]{2,1,0:T(8,128)(2,1)} %param.18) | copy-start | bytes 196612
  77.7 45.5 %copy-start.7 = (s32[1,32]{1,0:T(1,128)S(1)}, s32[1,32]{1,0:T(1,128)}, u32[]{:S(2)}) copy-start(s32[1,32]{1,0:T(1,128)} %param.22) | copy-start | bytes 388
  77.7 48.6 %copy-start.8 = (u32[256]{0:T(256)S(1)}, u32[256]{0:T(256)}, u32[]{:S(2)}) copy-start(u32[256]{0:T(256)} %constant.176) | copy-start | bytes 3076
  77.7 49.2 %copy-start.1 = (bf16[32,16,1024]{2,1,0:T(8,128)(2,1)S(1)}, bf16[32,16,1024]{2,1,0:T(8,128)(2,1)}, u32[]{:S(2)}) copy-start(bf16[32,16,1024]{2,1,0:T(8,128)(2,1)} %param.20) | copy-start | bytes 3145732
  77.7 49.2 %all-to-all-start = ((bf16[32,16,1024]{2,1,0:T(8,128)(2,1)}), bf16[32,16,1024]{2,1,0:T(8,128)(2,1)}, u32[]{:S(2)}, u32[]{:S(2)}) async-start(bf16[32,16,1024]{2,1,0:T(8,128)(2,1)} %select_multiply_fusion), calls=%async_computation | async-start | bytes 2097152 | tf_op jit(solution)/shard_map/all_to_all | solution.py:156
  228.8 263.2 %all-to-all-start.1 = ((bf16[2,32,1,128]{3,0,2,1:T(2,128)(2,1)}), bf16[2,32,1,128]{3,0,2,1:T(2,128)(2,1)S(1)}, u32[]{:S(2)}, u32[]{:S(2)}) async-start(bf16[2,32,1,128]{3,0,2,1:T(2,128)(2,1)} %copy.91), calls=%async_computation.1 | async-start | bytes 32768 | tf_op jit(solution)/shard_map/all_to_all | solution.py:143
  235.2 446.5 %reduce-scatter.2.cloned.1.call-start = ((), (), s32[]{:S(2)}) async-start(), calls=%async_computation.7 | async-start | bytes 2162688 | tf_op jit(solution)/shard_map/reduce_scatter | solution.py:168
Sparse Core Ops, SparseCore 0:
  9.1 55.8 all-gather.7
  71.7 82.5 all-gather.11
  156.8 68.9 all-gather.5
  228.2 263.7 all-reduce.2
  493.8 52.0 all-gather.9
  568.6 113.0 reduce-scatter.1
